TPU v7x, 256 devices: a whole 4x4x8 slice. The times are simulated.
256 devices in a mesh: prow: 8 (over z_hi, core), pcol: 32 (over x, z_lo, y).
Axes of the slice: x: 4, y: 4, z: 8 (z_hi: 4, z_lo: 2; z = z_hi * 2 + z_lo), core: 2. Of those that a mesh axis runs over, the one named last changes fastest.
Arguments:
- slab: float32 [2048, 98304], P('pcol', 'prow'), may hold values from -6 to 6
- vectors: float32 [98304, 512], P(('prow', 'pcol')), may hold values from -0.01953125 to 0.01953125
- tfactors: float32 [4, 128, 128], replicated, as said below
Outputs:
- transformed: float32 [2048, 98304], P('pcol', 'prow')
Inputs may be any that keep to these rules, and one draw needn't show every extreme that they name: Each tfactors[k] is upper triangular with diagonal entries between 1 and 2.
All inputs are finite; a program needn't handle non-finite values.
Results may differ from a plain program's by a relative error of at most 0.0001.
Values sent between devices are 32-bit elements; how exact they have to be, the bound alone decides.
No kernel may reach another device: no remote copies, remote signals or barrier semaphores. Data moves between devices by JAX's collectives and lax.ppermute only.
A program may use at most 128 MiB of HBM per device.

v0:
```python
import jax
import jax.numpy as jnp
from jax import lax
from jax.sharding import Mesh
from jax.sharding import PartitionSpec as P

PCOL_PARTS = (4, 2, 4)
GROUP = ("zl", "y")


def matmul(left, right):
    return jnp.dot(left, right, precision=lax.Precision.HIGHEST, preferred_element_type=jnp.float32)


def per_device(slab, vectors, tfactors):
    rows, cols = slab.shape
    depth = vectors.shape[0]
    count = tfactors.shape[0]
    width = tfactors.shape[1]
    nx = PCOL_PARTS[0]
    ng = PCOL_PARTS[1] * PCOL_PARTS[2]
    gram = lax.psum(
        matmul(vectors[:, width:].T, vectors[:, : (count - 1) * width]), ("prow", "x", "zl", "y")
    )
    basis = lax.all_gather(vectors, "x", axis=0, tiled=True)
    work = slab.reshape(rows, nx, ng, depth).transpose(2, 0, 1, 3)
    work = lax.all_to_all(work, GROUP, 0, 0, tiled=True).reshape(ng * rows, nx * depth)
    products = lax.psum(matmul(work, basis), ("zl", "y", "prow"))
    scaled = [None] * count
    for k in reversed(range(count)):
        part = products[:, k * width : (k + 1) * width]
        for j in range(k + 1, count):
            block = gram[(j - 1) * width : j * width, k * width : (k + 1) * width]
            part = part - matmul(scaled[j], block)
        scaled[k] = matmul(part, tfactors[k].T)
    scaled = jnp.concatenate(scaled, axis=1)
    work = work - matmul(scaled, basis.T)
    work = work.reshape(ng, rows, nx, depth)
    work = lax.all_to_all(work, GROUP, 0, 0, tiled=True)
    return work.transpose(1, 2, 0, 3).reshape(rows, cols)


def solution(mesh):
    devices = mesh.devices.reshape((mesh.shape["prow"],) + PCOL_PARTS)
    fine = Mesh(devices, ("prow", "x", "zl", "y"))
    cols = ("x", "zl", "y")
    in_specs = (P(cols, "prow"), P(("prow",) + cols, None), P())
    out_specs = P(cols, "prow")
    return jax.shard_map(
        per_device, mesh=fine, in_specs=in_specs, out_specs=out_specs, check_vma=False
    )
```

profile of v0, /device:TPU:2, one launch (start us, length us, event | category | flops | bytes accessed | tf_op | source)
XLA Modules:
  0.0 592.0 jit_solution(9328307342298171551)
XLA Ops:
  6.5 2.4 copy.6
  9.0 2.5 copy.10
  11.5 5.8 all-to-all-start
  17.3 0.0 all-gather.2.cloned.1.call-start
  17.3 0.7 all-gather.2.cloned.1.call-update
  18.0 0.0 all-reduce.3.cloned.1.call-start
  18.1 36.5 %all-to-all-done = f32[8,64,4,384]{3,2,1,0:T(4,128)S(1)} async-done(((f32[8,64,4,384]{3,2,1,0:T(4,128)}), f32[8,64,4,384]{3,2,1,0:T(4,128)S(1)}, u32[]{:S(2)}, u32[]{:S(2)}) %all-to-all-start) | async-done | bytes 3145760 | tf_op jit(solution)/shard_map/all_to_all | solution.py:27
  54.6 0.0 copy-start.1
  54.6 1.7 copy-done.1
  56.2 2.1 copy.7
  58.3 5.3 all-gather.2.cloned.1.call-done
  63.6 7.5 %fusion.30 = f32[512,512]{1,0:T(8,128)} fusion(f32[512,1536]{1,0:T(8,128)S(1)} %bitcast.37, f32[1536,512]{1,0:T(8,128)} %all-gather.2.cloned.1.call-done), kind=kOutput, calls=%fused_computation.38 | convolution fusion | flops 4831838208 | bytes 7340032 | tf_op jit(solution)/shard_map/dot_general | solution.py:12
  71.1 0.0 all-reduce.3.cloned.1.call-update
  71.1 0.2 all-reduce.5.cloned.1.call-start
  71.3 3.4 fusion.7
  74.7 0.0 all-reduce.5.cloned.1.call-update
  74.8 182.7 %all-reduce.3.cloned.1.call-done = f32[512,512]{1,0:T(8,128)} async-done(((f32[512,512]{1,0:T(8,128)}), f32[512,512]{1,0:T(8,128)}) %all-reduce.3.cloned.1.call-update) | async-done | bytes 1048592 | tf_op jit(solution)/shard_map/psum | solution.py:28
  257.4 1.3 fusion.10
  258.8 252.0 %all-reduce.5.cloned.1.call-done = f32[384,384]{1,0:T(8,128)} async-done(((f32[384,384]{1,0:T(8,128)}), f32[384,384]{1,0:T(8,128)}) %all-reduce.5.cloned.1.call-update) | async-done | bytes 589840 | tf_op jit(solution)/shard_map/psum | solution.py:22
  510.8 0.0 copy-start.2
  510.8 1.6 convolution_subtract_fusion.6
  512.4 0.0 copy-start
  512.4 1.4 fusion.22
  513.8 1.6 convolution_subtract_fusion.5
  515.4 1.4 convolution_subtract_fusion.4
  516.8 0.0 copy-done.2
  516.8 0.4 fusion.20
  517.2 1.6 convolution_subtract_fusion.3
  518.8 1.4 convolution_subtract_fusion.2
  520.3 1.4 convolution_subtract_fusion.1
  521.7 0.4 fusion.18
  522.1 0.0 copy-done
  522.1 12.2 %convolution_subtract_fusion = f32[512,1536]{1,0:T(8,128)} fusion(f32[512,1536]{1,0:T(8,128)S(1)} %bitcast.38, f32[1536,512]{1,0:T(8,128)S(1)} %copy-done, f32[512,128]{0,1:T(8,128)S(1)} %fusion.10, f32[512,128]{0,1:T(8,128)S(1)} %fusion.22, f32[512,128]{0,1:T(8,128)S(1)} %fusion.20, f32[512,128]{0,1:T(8,128)S(1)} %fusion.18), kind=kOutput, calls=%fused_computation | convolution fusion | flops 4833411072 | bytes 10485760 | tf_op jit(solution)/shard_map/dot_general | solution.py:12
  534.3 3.2 reshape.14
  537.5 42.7 %all_to_all.10 = f32[8,64,4,384]{3,2,1,0:T(4,128)S(1)} all-to-all(f32[8,64,4,384]{3,2,1,0:T(4,128)S(1)} %reshape.14), channel_id=1, replica_groups=mesh['prow'=8,'x'=4,'zl'=2,'y'=4] {'zl','y'}, dimensions={0} | all-to-all | bytes 6291456 | tf_op jit(solution)/shard_map/all_to_all | solution.py:39
  580.2 1.8 copy.5
  582.0 3.4 copy.8
Async XLA Ops:
  11.5 43.1 %all-to-all-start = ((f32[8,64,4,384]{3,2,1,0:T(4,128)}), f32[8,64,4,384]{3,2,1,0:T(4,128)S(1)}, u32[]{:S(2)}, u32[]{:S(2)}) async-start(f32[8,64,4,384]{3,2,1,0:T(4,128)} %bitcast.40), calls=%async_computation | async-start | bytes 6291456 | tf_op jit(solution)/shard_map/all_to_all | solution.py:27
  17.3 46.3 %all-gather.2.cloned.1.call-start = ((), (), s32[]{:S(2)}) async-start(), calls=%async_computation.2 | async-start | bytes 3932160 | tf_op jit(solution)/shard_map/all_gather | solution.py:25
  18.0 239.4 %all-reduce.3.cloned.1.call-start = ((), (), s32[]{:S(2)}) async-start(), calls=%async_computation.3 | async-start | bytes 2097152 | tf_op jit(solution)/shard_map/psum | solution.py:28
  54.6 1.7 copy-start.1
  71.1 439.6 %all-reduce.5.cloned.1.call-start = ((), (), s32[]{:S(2)}) async-start(), calls=%async_computation.4 | async-start | bytes 1179648 | tf_op jit(solution)/shard_map/psum | solution.py:22
  510.8 6.1 %copy-start.2 = (f32[4,128,128]{2,1,0:T(8,128)S(1)}, f32[4,128,128]{2,1,0:T(8,128)}, u32[]{:S(2)}) copy-start(f32[4,128,128]{2,1,0:T(8,128)} %param.5) | copy-start | bytes 786436
  512.4 9.7 %copy-start = (f32[1536,512]{1,0:T(8,128)S(1)}, f32[1536,512]{1,0:T(8,128)}, u32[]{:S(2)}) copy-start(f32[1536,512]{1,0:T(8,128)} %all-gather.2.cloned.1.call-done) | copy-start | bytes 9437188
Sparse Core Ops, SparseCore 0:
  19.9 43.6 all-gather.1
  71.2 186.1 all-reduce.2
  263.9 246.8 all-reduce.4
where the time goes:
time: 593 us; the launch traced here: 592 us
  waiting for transfers between devices  477 us (80%)
  blocking collectives  42.7 us (7%)
  matrix products  35.6 us (6%)
  local copies, waits for them, and re-layouts  17.1 us (3%)
  between operations  13.2 us (2%)
  starting transfers between devices  6.12 us (1%)
    psum x1, waiting for transfers between devices, per_device(): lax.psum(matmul(vectors[:, width:].T, vectors[:, :(count - 1) * width]),...  252 us
    psum x1, waiting for transfers between devices, per_device(): products = lax.psum(matmul(work, basis), ('zl', 'y', 'prow'))  183 us
    all_to_all x1, blocking collectives, per_device(): work = lax.all_to_all(work, GROUP, 0, 0, tiled=True)  42.7 us
    all_to_all x1, waiting for transfers between devices, per_device(): lax.all_to_all(work, GROUP, 0, 0, tiled=True).reshape(ng * rows, nx * depth)  36.5 us
    dot_general x13, matrix products, matmul(): jnp.dot(left, right, precision=lax.Precision.HIGHEST, preferred_element_t...  35.6 us
  transfers between devices with their start and end apart: 4, of which 4 were waited for; matrix products, arithmetic and copies ran while one was open for 1% of the time, Pallas kernels for 0%

commit v1 on v0

--- a/solution.py
+++ b/solution.py
@@ -25,7 +25,9 @@
     basis = lax.all_gather(vectors, "x", axis=0, tiled=True)
     work = slab.reshape(rows, nx, ng, depth).transpose(2, 0, 1, 3)
     work = lax.all_to_all(work, GROUP, 0, 0, tiled=True).reshape(ng * rows, nx * depth)
-    products = lax.psum(matmul(work, basis), ("zl", "y", "prow"))
+    own = matmul(work, basis)
+    terms = lax.all_gather(own, ("zl", "y", "prow"))
+    products = jnp.sum(terms, axis=0)
     scaled = [None] * count
     for k in reversed(range(count)):
         part = products[:, k * width : (k + 1) * width]

time: 593 us -> 648 us (1.093)
  waiting for transfers between devices: 477 us -> 509 us
  other arithmetic: 0 us -> 22.1 us
    all_gather x0 -> x1, waiting for transfers between devices: none -> 365 us  [per_device(): terms = lax.all_gather(own, ('zl', 'y', 'prow'))]
    psum x1 -> x0, waiting for transfers between devices: 183 us -> none  [per_device(): products = lax.psum(matmul(work, basis), ('zl', 'y', 'prow'))]
    psum x1, waiting for transfers between devices: 252 us -> 102 us  [per_device(): lax.psum(matmul(vectors[:, width:].T, vectors[:, :(count - 1) * width]),...]
    reduce_sum x0 -> x1, other arithmetic: none -> 22.1 us  [per_device(): products = jnp.sum(terms, axis=0)]
  transfers between devices with their start and end apart: 4 -> 4, of which waited for: 4 -> 4; matrix products, arithmetic and copies ran while one was open for 1% -> 4% of each run, Pallas kernels for 0% -> 0%
where the time goes in v1:
time: 648 us
  waiting for transfers between devices  509 us (79%)
  blocking collectives  42.8 us (7%)
  matrix products  35.6 us (5%)
  other arithmetic  22.1 us (3%)
  local copies, waits for them, and re-layouts  17.1 us (3%)
  between operations  15 us (2%)
    all_gather x1, waiting for transfers between devices, per_device(): terms = lax.all_gather(own, ('zl', 'y', 'prow'))  365 us
    psum x1, waiting for transfers between devices, per_device(): lax.psum(matmul(vectors[:, width:].T, vectors[:, :(count - 1) * width]),...  102 us
    all_to_all x1, blocking collectives, per_device(): work = lax.all_to_all(work, GROUP, 0, 0, tiled=True)  42.8 us
    all_to_all x1, waiting for transfers between devices, per_device(): lax.all_to_all(work, GROUP, 0, 0, tiled=True).reshape(ng * rows, nx * depth)  36.5 us
    dot_general x13, matrix products, matmul(): jnp.dot(left, right, precision=lax.Precision.HIGHEST, preferred_element_t...  35.6 us
    reduce_sum x1, other arithmetic, per_device(): products = jnp.sum(terms, axis=0)  22.1 us
  transfers between devices with their start and end apart: 4, of which 4 were waited for; matrix products, arithmetic and copies ran while one was open for 4% of the time, Pallas kernels for 0%

profile of v1, /device:TPU:2, one launch (start us, length us, event | category | flops | bytes accessed | tf_op | source)
XLA Modules:
  0.0 647.5 jit_solution(15395744205558190033)
XLA Ops:
  7.4 2.4 copy.6
  9.8 2.5 copy.10
  12.3 5.8 all-to-all-start
  18.1 0.0 all-gather.4.cloned.1.call-start
  18.2 0.7 all-gather.4.cloned.1.call-update
  18.8 0.0 all-gather.6.cloned.1.call-start
  18.9 36.5 %all-to-all-done = f32[8,64,4,384]{3,2,1,0:T(4,128)S(1)} async-done(((f32[8,64,4,384]{3,2,1,0:T(4,128)}), f32[8,64,4,384]{3,2,1,0:T(4,128)S(1)}, u32[]{:S(2)}, u32[]{:S(2)}) %all-to-all-start) | async-done | bytes 3145760 | tf_op jit(solution)/shard_map/all_to_all | solution.py:27
  55.4 0.0 copy-start.1
  55.4 1.7 copy-done.1
  57.1 2.1 copy.7
  59.2 5.3 all-gather.4.cloned.1.call-done
  64.5 7.5 %fusion.30 = f32[512,512]{1,0:T(8,128)} fusion(f32[512,1536]{1,0:T(8,128)S(1)} %bitcast.38, f32[1536,512]{1,0:T(8,128)} %all-gather.4.cloned.1.call-done), kind=kOutput, calls=%fused_computation.38 | convolution fusion | flops 4831838208 | bytes 7340032 | tf_op jit(solution)/shard_map/dot_general | solution.py:12
  71.9 0.0 all-gather.6.cloned.1.call-update
  72.0 0.0 all-reduce.2.cloned.1.call-start
  72.0 3.4 fusion.7
  75.4 0.0 all-reduce.2.cloned.1.call-update
  75.4 364.8 %all-gather.6.cloned.1.call-done = f32[32768,512]{1,0:T(8,128)} async-done(((f32[512,512]{1,0:T(8,128)}), f32[32768,512]{1,0:T(8,128)}) %all-gather.6.cloned.1.call-update) | async-done | bytes 67108880 | tf_op jit(solution)/shard_map/all_gather | solution.py:29
  440.2 22.1 %reduce_sum.9 = f32[512,512]{1,0:T(8,128)} reduce(f32[64,512,512]{2,1,0:T(8,128)} %bitcast.1, f32[]{:T(128)} %constant.0.clone.1), dimensions={0}, to_apply=%region_0.0 | reduce | flops 16515072 | bytes 68157440 | tf_op jit(solution)/shard_map/reduce_sum | solution.py:30
  462.3 1.3 fusion.10
  463.7 101.6 %all-reduce.2.cloned.1.call-done = f32[384,384]{1,0:T(8,128)} async-done(((f32[384,384]{1,0:T(8,128)}), f32[384,384]{1,0:T(8,128)}) %all-reduce.2.cloned.1.call-update) | async-done | bytes 589840 | tf_op jit(solution)/shard_map/psum | solution.py:22
  565.3 0.0 copy-start.2
  565.3 1.6 convolution_subtract_fusion.6
  566.9 0.0 copy-start
  566.9 1.4 fusion.22
  568.3 1.6 convolution_subtract_fusion.5
  569.9 1.4 convolution_subtract_fusion.4
  571.3 0.0 copy-done.2
  571.4 0.4 fusion.20
  571.7 1.6 convolution_subtract_fusion.3
  573.3 1.4 convolution_subtract_fusion.2
  574.8 1.4 convolution_subtract_fusion.1
  576.2 0.4 fusion.18
  576.6 0.0 copy-done
  576.6 12.2 %convolution_subtract_fusion = f32[512,1536]{1,0:T(8,128)} fusion(f32[512,1536]{1,0:T(8,128)S(1)} %bitcast.39, f32[1536,512]{1,0:T(8,128)S(1)} %copy-done, f32[512,128]{0,1:T(8,128)S(1)} %fusion.10, f32[512,128]{0,1:T(8,128)S(1)} %fusion.22, f32[512,128]{0,1:T(8,128)S(1)} %fusion.20, f32[512,128]{0,1:T(8,128)S(1)} %fusion.18), kind=kOutput, calls=%fused_computation | convolution fusion | flops 4833411072 | bytes 10485760 | tf_op jit(solution)/shard_map/dot_general | solution.py:12
  588.8 3.2 reshape.14
  592.0 42.8 %all_to_all.10 = f32[8,64,4,384]{3,2,1,0:T(4,128)S(1)} all-to-all(f32[8,64,4,384]{3,2,1,0:T(4,128)S(1)} %reshape.14), channel_id=1, replica_groups=mesh['prow'=8,'x'=4,'zl'=2,'y'=4] {'zl','y'}, dimensions={0} | all-to-all | bytes 6291456 | tf_op jit(solution)/shard_map/all_to_all | solution.py:41
  634.8 1.8 copy.5
  636.6 3.4 copy.8
Async XLA Ops:
  12.3 43.1 %all-to-all-start = ((f32[8,64,4,384]{3,2,1,0:T(4,128)}), f32[8,64,4,384]{3,2,1,0:T(4,128)S(1)}, u32[]{:S(2)}, u32[]{:S(2)}) async-start(f32[8,64,4,384]{3,2,1,0:T(4,128)} %bitcast.41), calls=%async_computation | async-start | bytes 6291456 | tf_op jit(solution)/shard_map/all_to_all | solution.py:27
  18.1 46.3 %all-gather.4.cloned.1.call-start = ((), (), s32[]{:S(2)}) async-start(), calls=%async_computation.2 | async-start | bytes 3932160 | tf_op jit(solution)/shard_map/all_gather | solution.py:25
  18.8 421.4 %all-gather.6.cloned.1.call-start = ((), (), s32[]{:S(2)}) async-start(), calls=%async_computation.4 | async-start | bytes 68157440 | tf_op jit(solution)/shard_map/all_gather | solution.py:29
  55.4 1.7 copy-start.1
  72.0 493.3 %all-reduce.2.cloned.1.call-start = ((), (), s32[]{:S(2)}) async-start(), calls=%async_computation.3 | async-start | bytes 1179648 | tf_op jit(solution)/shard_map/psum | solution.py:22
  565.3 6.1 copy-start.2
  566.9 9.7 %copy-start = (f32[1536,512]{1,0:T(8,128)S(1)}, f32[1536,512]{1,0:T(8,128)}, u32[]{:S(2)}) copy-start(f32[1536,512]{1,0:T(8,128)} %all-gather.4.cloned.1.call-done) | copy-start | bytes 9437188
Sparse Core Ops, SparseCore 0:
  20.8 43.6 all-gather.3
  72.1 368.1 all-gather.5
Sparse Core Ops, SparseCore 1:
  77.9 487.3 all-reduce.1
